TPU v7x, 128 devices: a whole 4x4x4 slice. The times are simulated.
128 devices in a mesh: row: 4 (over z), col: 32 (over x, y, core).
Axes of the slice: x: 4, y: 4, z: 4, core: 2. Of those that a mesh axis runs over, the one named last changes fastest.
Arguments:
- matrix_real: bfloat16 [512, 16384], P('col', 'row'), may hold values from -0.25 to 0.25
- matrix_imag: bfloat16 [512, 16384], P('col', 'row'), may hold values from -0.25 to 0.25
- valence_index: int32 [512], P('col'), may hold values from 0 to 15
- conduction_index: int32 [512], P('col'), may hold values from 0 to 31
- valence_energy: float32 [16], replicated, may hold values from -1.5 to -0.1
- conduction_energy: float32 [32], replicated, may hold values from 0.1 to 2
- frequency: float32 [2], replicated, may hold values from 0.2 to 2
Outputs:
- chi_real: bfloat16 [2, 16384, 16384], P(None, 'row', 'col')
- chi_imag: bfloat16 [2, 16384, 16384], P(None, 'row', 'col')
All inputs are finite; a program needn't handle non-finite values.
Results may differ from a plain program's by a relative error of at most 0.005.
Values may be sent and summed in bfloat16 or wider, within the bound.
No kernel may reach another device: no remote copies, remote signals or barrier semaphores. Data moves between devices by JAX's collectives and lax.ppermute only.
A program may use at most 192 MiB of HBM per device.

v0:
```python
import jax
import jax.numpy as jnp
from jax import lax
from jax.sharding import PartitionSpec as P


def lookup(indices, table):
    count = table.shape[0]
    picks = indices[:, None] == lax.broadcasted_iota(jnp.int32, (1, count), 1)
    return jnp.sum(jnp.where(picks, table[None, :], 0.0), axis=1)


def contract(left_side, right_side):
    return lax.dot_general(
        left_side, right_side, (((0,), (0,)), ((), ())), preferred_element_type=jnp.float32
    )


CHUNKS = 4


def on_device(
    matrix_real,
    matrix_imag,
    valence_index,
    conduction_index,
    valence_energy,
    conduction_energy,
    frequency,
):
    ncol = lax.psum(1, "col")
    local_pairs, local_g = matrix_real.shape
    pairs = local_pairs * ncol
    both = jnp.stack([matrix_real, matrix_imag])
    bands = jnp.stack([valence_index, conduction_index]).astype(jnp.float32)
    all_bands = lax.all_gather(bands, "col", axis=1, tiled=True).astype(jnp.int32)
    gap = lookup(all_bands[1], conduction_energy) - lookup(all_bands[0], valence_energy)
    spread = lax.all_gather(both, "row", axis=2, tiled=True)
    spread = spread.reshape(2, local_pairs, ncol, -1)
    column = lax.all_to_all(spread, "col", split_axis=2, concat_axis=1, tiled=True)
    width = column.shape[-1]
    wide = column.reshape(2, pairs, width).astype(jnp.float32)
    right_real = []
    right_imag = []
    for index in range(frequency.shape[0]):
        omega = frequency[index]
        weight = 4.0 * gap / (gap * gap + omega * omega)
        scaled_real = (weight[:, None] * wide[0]).astype(jnp.bfloat16)
        scaled_imag = (weight[:, None] * wide[1]).astype(jnp.bfloat16)
        right_real.append(jnp.concatenate([-scaled_real, -scaled_imag], axis=0))
        right_imag.append(jnp.concatenate([-scaled_imag, scaled_real], axis=0))
    step = local_g // CHUNKS
    real_parts = [[] for _ in right_real]
    imag_parts = [[] for _ in right_real]
    for chunk in range(CHUNKS):
        piece = both[:, :, chunk * step : (chunk + 1) * step]
        left = lax.all_gather(piece, "col", axis=1, tiled=True).reshape(2 * pairs, step)
        for index in range(len(right_real)):
            real_parts[index].append(contract(left, right_real[index]).astype(jnp.bfloat16))
            imag_parts[index].append(contract(left, right_imag[index]).astype(jnp.bfloat16))
    chi_real = jnp.stack([jnp.concatenate(p, axis=0) for p in real_parts])
    chi_imag = jnp.stack([jnp.concatenate(p, axis=0) for p in imag_parts])
    return (chi_real, chi_imag)


def solution(mesh):
    placed = (P("col", "row"), P("col", "row"), P("col"), P("col"), P(), P(), P())
    return jax.shard_map(
        on_device,
        mesh=mesh,
        in_specs=placed,
        out_specs=(P(None, "row", "col"), P(None, "row", "col")),
        check_vma=False,
    )
```

profile of v0, /device:TPU:1, one launch (start us, length us, event | category | flops | bytes accessed | tf_op | source)
XLA Modules:
  0.0 271.8 jit_solution(17406845412309366294)
XLA Ops:
  7.2 1.7 pad_maximum_fusion.6
  11.9 24.9 %all-gather.9.cloned.1.call-done = bf16[2,16,16384]{2,1,0:T(8,128)(2,1)} async-done(((bf16[2,16,4096]{2,1,0:T(8,128)(2,1)}), bf16[2,16,16384]{2,1,0:T(8,128)(2,1)}) %all-gather.9.cloned.1.call-update) | async-done | bytes 1048592 | tf_op jit(solution)/shard_map/all_gather | solution.py:38
  36.8 2.4 copy.26
  39.2 8.4 %all-to-all-start = ((bf16[2,16,32,512]{3,1,0,2:T(8,128)(2,1)}), bf16[2,16,32,512]{3,1,0,2:T(8,128)(2,1)S(1)}, u32[]{:S(2)}, u32[]{:S(2)}) async-start(bf16[2,16,32,512]{3,1,0,2:T(8,128)(2,1)} %bitcast.71), calls=%async_computation | async-start | bytes 2097152 | tf_op jit(solution)/shard_map/all_to_all | solution.py:40
  51.3 29.0 %all-gather = f32[32,16,2]{1,2,0:T(2,128)S(1)} all-gather(f32[1,16,2]{1,2,0:T(2,128)S(1)} %fusion.10), channel_id=1, replica_groups=mesh['row'=4,'col'=32] {'col'}, dimensions={0}, use_global_device_ids=true | all-gather | bytes 4224 | tf_op jit(solution)/shard_map/all_gather | solution.py:36
  82.7 5.7 %all-gather.11.cloned.1.call-done = bf16[2,512,1024]{2,1,0:T(8,128)(2,1)} async-done(((bf16[2,16,1024]{2,1,0:T(8,128)(2,1)}), bf16[2,512,1024]{2,1,0:T(8,128)(2,1)}) %all-gather.11.cloned.1.call-update) | async-done | bytes 2097168 | tf_op jit(solution)/shard_map/all_gather | solution.py:57
  88.4 3.8 %convolution_convert_fusion.10 = bf16[1024,512]{1,0:T(8,128)(2,1)} fusion(bf16[1024,1024]{1,0:T(8,128)(2,1)} %bitcast.82, bf16[512,512]{1,0:T(8,128)(2,1)S(1)} %get-tuple-element.11, bf16[512,512]{1,0:T(8,128)(2,1)S(1)} %get-tuple-element.16), kind=kOutput, calls=%fused_computation.17 | convolution fusion | flops 1076363264 | bytes 4194304 | tf_op jit(solution)/shard_map/dot_general | solution.py:14
  92.3 41.5 %all-gather.7.cloned.1.call-done = bf16[2,512,1024]{2,1,0:T(8,128)(2,1)} async-done(((bf16[2,16,1024]{2,1,0:T(8,128)(2,1)}), bf16[2,512,1024]{2,1,0:T(8,128)(2,1)}) %all-gather.7.cloned.1.call-update) | async-done | bytes 2097168 | tf_op jit(solution)/shard_map/all_gather | solution.py:57
  133.8 4.0 %convolution_convert_fusion.11 = bf16[1024,512]{1,0:T(8,128)(2,1)} fusion(bf16[1024,1024]{1,0:T(8,128)(2,1)} %bitcast.86, bf16[512,512]{1,0:T(8,128)(2,1)S(1)} %get-tuple-element.11, bf16[512,512]{1,0:T(8,128)(2,1)S(1)} %get-tuple-element.16), kind=kOutput, calls=%fused_computation.18 | convolution fusion | flops 1076363264 | bytes 4194304 | tf_op jit(solution)/shard_map/dot_general | solution.py:14
  139.3 2.5 convolution_convert_fusion.2
  141.9 37.1 %all-gather.13.cloned.1.call-done = bf16[2,512,1024]{2,1,0:T(8,128)(2,1)} async-done(((bf16[2,16,1024]{2,1,0:T(8,128)(2,1)}), bf16[2,512,1024]{2,1,0:T(8,128)(2,1)}) %all-gather.13.cloned.1.call-update) | async-done | bytes 2097168 | tf_op jit(solution)/shard_map/all_gather | solution.py:57
  179.0 4.2 %convolution_convert_fusion.9 = bf16[1024,512]{1,0:T(8,128)(2,1)} fusion(bf16[1024,1024]{1,0:T(8,128)(2,1)} %bitcast.90, bf16[512,512]{1,0:T(8,128)(2,1)} %copy-done.5, bf16[512,512]{1,0:T(8,128)(2,1)} %copy-done.11), kind=kOutput, calls=%fused_computation.16 | convolution fusion | flops 1076363264 | bytes 4194304 | tf_op jit(solution)/shard_map/dot_general | solution.py:14
  183.2 2.3 convolution_convert_fusion.1
  185.5 38.7 %all-gather.15.cloned.1.call-done = bf16[2,512,1024]{2,1,0:T(8,128)(2,1)} async-done(((bf16[2,16,1024]{2,1,0:T(8,128)(2,1)}), bf16[2,512,1024]{2,1,0:T(8,128)(2,1)}) %all-gather.15.cloned.1.call-update) | async-done | bytes 2097168 | tf_op jit(solution)/shard_map/all_gather | solution.py:57
  224.2 3.3 %convolution_convert_fusion.8 = bf16[1024,512]{1,0:T(8,128)(2,1)S(1)} fusion(bf16[1024,1024]{1,0:T(8,128)(2,1)} %bitcast.94, bf16[512,512]{1,0:T(8,128)(2,1)} %copy-done.5, bf16[512,512]{1,0:T(8,128)(2,1)} %copy-done.11), kind=kOutput, calls=%fused_computation.15 | convolution fusion | flops 1076363264 | bytes 4194304 | tf_op jit(solution)/shard_map/dot_general | solution.py:14
  227.5 2.3 convolution_convert_fusion
  232.7 2.5 convolution_convert_fusion.6
  235.2 2.3 convolution_convert_fusion.5
  238.8 2.4 convolution_convert_fusion.4
  241.2 2.3 convolution_convert_fusion.7
  245.3 2.8 %maximum_bitcast_fusion = (bf16[1,4096,512]{2,1,0:T(8,128)(2,1)S(1)}, bf16[1,4096,512]{2,1,0:T(8,128)(2,1)}) fusion(bf16[1024,512]{1,0:T(8,128)(2,1)S(1)} %convolution_convert_fusion.12, bf16[1024,512]{1,0:T(8,128)(2,1)S(1)} %convolution_convert_fusion.13, bf16[1024,512]{1,0:T(8,128)(2,1)S(1)} %convolution_convert_fusion.14, ...), kind=kLoop, calls=%fused_computation.2 | loop fusion | flops 33554432 | bytes 16777216 | tf_op jit(solution)/shard_map/stack | solution.py:61
  248.1 6.3 %pad_maximum_fusion = bf16[2,4096,512]{2,1,0:T(8,128)(2,1)} fusion(bf16[1,4096,512]{2,1,0:T(8,128)(2,1)} %get-tuple-element.27, bf16[1,4096,512]{2,1,0:T(8,128)(2,1)S(1)} %get-tuple-element.26), kind=kLoop, calls=%fused_computation | loop fusion | flops 4194304 | bytes 16777216 | tf_op jit(solution)/shard_map/stack | solution.py:61
  254.5 4.4 %maximum_bitcast_fusion.2 = (bf16[1,4096,512]{2,1,0:T(8,128)(2,1)S(1)}, bf16[1,4096,512]{2,1,0:T(8,128)(2,1)}) fusion(bf16[1024,512]{1,0:T(8,128)(2,1)} %convolution_convert_fusion.4, bf16[1024,512]{1,0:T(8,128)(2,1)} %convolution_convert_fusion.5, bf16[1024,512]{1,0:T(8,128)(2,1)} %convolution_convert_fusion.6, ...), kind=kLoop, calls=%fused_computation.4 | loop fusion | flops 33554432 | bytes 16777216 | tf_op jit(solution)/shard_map/stack | solution.py:62
  258.9 6.3 %pad_maximum_fusion.1 = bf16[2,4096,512]{2,1,0:T(8,128)(2,1)} fusion(bf16[1,4096,512]{2,1,0:T(8,128)(2,1)} %get-tuple-element.29, bf16[1,4096,512]{2,1,0:T(8,128)(2,1)S(1)} %get-tuple-element.28), kind=kLoop, calls=%fused_computation.1 | loop fusion | flops 4194304 | bytes 16777216 | tf_op jit(solution)/shard_map/stack | solution.py:62
  (78 shorter events, 14.1 us)
Async XLA Ops:
  7.2 29.6 %all-gather.9.cloned.1.call-start = ((), (), s32[]{:S(2)}) async-start(), calls=%async_computation.2 | async-start | bytes 1310720 | tf_op jit(solution)/shard_map/all_gather | solution.py:38
  8.9 79.5 %all-gather.11.cloned.1.call-start = ((), (), s32[]{:S(2)}) async-start(), calls=%async_computation.3 | async-start | bytes 2162688 | tf_op jit(solution)/shard_map/all_gather | solution.py:57
  10.6 123.2 %all-gather.7.cloned.1.call-start = ((), (), s32[]{:S(2)}) async-start(), calls=%async_computation.1 | async-start | bytes 2162688 | tf_op jit(solution)/shard_map/all_gather | solution.py:57
  11.3 167.7 %all-gather.13.cloned.1.call-start = ((), (), s32[]{:S(2)}) async-start(), calls=%async_computation.4 | async-start | bytes 2162688 | tf_op jit(solution)/shard_map/all_gather | solution.py:57
  36.8 11.5 %copy-start.12 = (f32[2]{0:T(128)S(1)}, f32[2]{0:T(128)}, u32[]{:S(2)}) copy-start(f32[2]{0:T(128)} %param.13) | copy-start | bytes 28
  36.8 14.5 %copy-start.15 = (s32[16]{0:T(128)S(1)}, s32[16]{0:T(128)}, u32[]{:S(2)}) copy-start(s32[16]{0:T(128)} %param.10) | copy-start | bytes 196
  36.8 14.5 %copy-start.16 = (s32[16]{0:T(128)S(1)}, s32[16]{0:T(128)}, u32[]{:S(2)}) copy-start(s32[16]{0:T(128)} %param.9) | copy-start | bytes 196
  36.8 43.8 %copy-start.13 = (f32[16]{0:T(128)S(1)}, f32[16]{0:T(128)}, u32[]{:S(2)}) copy-start(f32[16]{0:T(128)} %param.11) | copy-start | bytes 196
  36.8 43.9 %copy-start.14 = (f32[32]{0:T(128)S(1)}, f32[32]{0:T(128)}, u32[]{:S(2)}) copy-start(f32[32]{0:T(128)} %param.12) | copy-start | bytes 388
  39.2 41.6 %all-to-all-start = ((bf16[2,16,32,512]{3,1,0,2:T(8,128)(2,1)}), bf16[2,16,32,512]{3,1,0,2:T(8,128)(2,1)S(1)}, u32[]{:S(2)}, u32[]{:S(2)}) async-start(bf16[2,16,32,512]{3,1,0,2:T(8,128)(2,1)} %bitcast.71), calls=%async_computation | async-start | bytes 2097152 | tf_op jit(solution)/shard_map/all_to_all | solution.py:40
  47.6 176.6 %all-gather.15.cloned.1.call-start = ((), (), s32[]{:S(2)}) async-start(), calls=%async_computation.5 | async-start | bytes 2162688 | tf_op jit(solution)/shard_map/all_gather | solution.py:57
  82.7 51.0 %copy-start.11 = (bf16[512,512]{1,0:T(8,128)(2,1)}, bf16[512,512]{1,0:T(8,128)(2,1)S(1)}, u32[]{:S(2)}) copy-start(bf16[512,512]{1,0:T(8,128)(2,1)S(1)} %get-tuple-element.16) | copy-start | bytes 1572868
  82.7 55.0 %copy-start.5 = (bf16[512,512]{1,0:T(8,128)(2,1)}, bf16[512,512]{1,0:T(8,128)(2,1)S(1)}, u32[]{:S(2)}) copy-start(bf16[512,512]{1,0:T(8,128)(2,1)S(1)} %get-tuple-element.11) | copy-start | bytes 1572868
  82.7 55.0 %copy-start.8 = (bf16[512,512]{1,0:T(8,128)(2,1)}, bf16[512,512]{1,0:T(8,128)(2,1)S(1)}, u32[]{:S(2)}) copy-start(bf16[512,512]{1,0:T(8,128)(2,1)S(1)} %get-tuple-element.17) | copy-start | bytes 1572868
  133.7 4.0 %copy-start.19 = (bf16[2,512,1024]{2,1,0:T(8,128)(2,1)S(1)}, bf16[2,512,1024]{2,1,0:T(8,128)(2,1)}, u32[]{:S(2)}) copy-start(bf16[2,512,1024]{2,1,0:T(8,128)(2,1)} %all-gather.7.cloned.1.call-done) | copy-start | bytes 6291460
  179.0 4.2 %copy-start.6 = (bf16[512,512]{1,0:T(8,128)(2,1)S(1)}, bf16[512,512]{1,0:T(8,128)(2,1)}, u32[]{:S(2)}) copy-start(bf16[512,512]{1,0:T(8,128)(2,1)} %copy-done.5) | copy-start | bytes 1572868
  179.0 4.2 %copy-start.9 = (bf16[512,512]{1,0:T(8,128)(2,1)S(1)}, bf16[512,512]{1,0:T(8,128)(2,1)}, u32[]{:S(2)}) copy-start(bf16[512,512]{1,0:T(8,128)(2,1)} %copy-done.8) | copy-start | bytes 1572868
  179.0 4.2 %copy-start.21 = (bf16[2,512,1024]{2,1,0:T(8,128)(2,1)S(1)}, bf16[2,512,1024]{2,1,0:T(8,128)(2,1)}, u32[]{:S(2)}) copy-start(bf16[2,512,1024]{2,1,0:T(8,128)(2,1)} %all-gather.13.cloned.1.call-done) | copy-start | bytes 6291460
  224.2 3.3 %copy-start.7 = (bf16[512,512]{1,0:T(8,128)(2,1)S(1)}, bf16[512,512]{1,0:T(8,128)(2,1)}, u32[]{:S(2)}) copy-start(bf16[512,512]{1,0:T(8,128)(2,1)} %copy-done.5) | copy-start | bytes 1572868
  224.2 3.3 %copy-start.10 = (bf16[512,512]{1,0:T(8,128)(2,1)S(1)}, bf16[512,512]{1,0:T(8,128)(2,1)}, u32[]{:S(2)}) copy-start(bf16[512,512]{1,0:T(8,128)(2,1)} %copy-done.8) | copy-start | bytes 1572868
  224.2 3.3 %copy-start.23 = (bf16[2,512,1024]{2,1,0:T(8,128)(2,1)S(1)}, bf16[2,512,1024]{2,1,0:T(8,128)(2,1)}, u32[]{:S(2)}) copy-start(bf16[2,512,1024]{2,1,0:T(8,128)(2,1)} %all-gather.15.cloned.1.call-done) | copy-start | bytes 6291460
  227.5 2.3 copy-start.3
  227.5 2.3 copy-start.18
  238.8 2.4 copy-start.20
  (6 other events, 9.2 us)
Sparse Core Ops, SparseCore 0:
  10.2 26.4 all-gather.8
  39.7 48.6 all-gather.10
  90.8 42.9 all-gather.6
  136.0 42.9 all-gather.12
  181.2 42.9 all-gather.14
where the time goes:
time: 272 us
  waiting for transfers between devices  150 us (55%)
  matrix products  38.2 us (14%)
  blocking collectives  29 us (11%)
  other arithmetic  25.1 us (9%)
  between operations  16.5 us (6%)
  starting transfers between devices  8.64 us (3%)
  local copies, waits for them, and re-layouts  4.61 us (2%)
    all_gather x4, waiting for transfers between devices, on_device(): lax.all_gather(piece, 'col', axis=1, tiled=True).reshape(2 * pairs, step)  123 us
    dot_general x16, matrix products, contract(): lax.dot_general(left_side, right_side, (((0,), (0,)), ((), ())), preferre...  38.2 us
    all_gather x1, blocking collectives, on_device(): lax.all_gather(bands, 'col', axis=1, tiled=True).astype(jnp.int32)  29 us
    all_gather x1, waiting for transfers between devices, on_device(): spread = lax.all_gather(both, 'row', axis=2, tiled=True)  24.9 us
    another operation x2, other arithmetic, on_device(): chi_imag = jnp.stack([jnp.concatenate(p, axis=0) for p in imag_parts])  10.8 us
    another operation x2, other arithmetic, on_device(): chi_real = jnp.stack([jnp.concatenate(p, axis=0) for p in real_parts])  9.18 us
    all_to_all x1, starting transfers between devices, on_device(): lax.all_to_all(spread, 'col', split_axis=2, concat_axis=1, tiled=True)  8.44 us
  transfers between devices with their start and end apart: 6, of which 5 were waited for; matrix products, arithmetic and copies ran while one was open for 9% of the time, Pallas kernels for 0%

commit v1 on v0

--- a/solution.py
+++ b/solution.py
@@ -2,6 +2,12 @@
 import jax.numpy as jnp
 from jax import lax
 from jax.sharding import PartitionSpec as P
+
+
+def laid_out(blocks, dim):
+    dims = list(blocks.shape[1:])
+    dims[dim] *= blocks.shape[0]
+    return jnp.moveaxis(blocks, 0, dim).reshape(dims)
 
 
 def lookup(indices, table):
@@ -35,7 +41,19 @@
     bands = jnp.stack([valence_index, conduction_index]).astype(jnp.float32)
     all_bands = lax.all_gather(bands, "col", axis=1, tiled=True).astype(jnp.int32)
     gap = lookup(all_bands[1], conduction_energy) - lookup(all_bands[0], valence_energy)
-    spread = lax.all_gather(both, "row", axis=2, tiled=True)
+    peers = lax.axis_size("row")
+    pairs_2 = [(i, (i + 1) % peers) for i in range(peers)]
+    back = [(b, a) for a, b in pairs_2]
+    lower, upper = ([], [])
+    for step_2 in range(peers - 1):
+        if step_2 % 2 == 0:
+            lower.append(lax.ppermute(lower[-1] if lower else both, "row", pairs_2))
+        else:
+            upper.append(lax.ppermute(upper[-1] if upper else both, "row", back))
+    blocks = jnp.stack([*lower[::-1], both, *upper])
+    shift = lax.axis_index("row") - len(lower)
+    blocks = blocks[(jnp.arange(peers) - shift) % peers]
+    spread = laid_out(blocks, 2)
     spread = spread.reshape(2, local_pairs, ncol, -1)
     column = lax.all_to_all(spread, "col", split_axis=2, concat_axis=1, tiled=True)
     width = column.shape[-1]

time: 272 us -> 248 us (0.912)
  waiting for transfers between devices: 150 us -> 116 us
  starting transfers between devices: 8.64 us -> 14.1 us
    all_gather x1 -> x0, waiting for transfers between devices: 24.9 us -> none  [on_device(): spread = lax.all_gather(both, 'row', axis=2, tiled=True)]
    all_gather x4, waiting for transfers between devices: 123 us -> 101 us  [on_device(): lax.all_gather(piece, 'col', axis=1, tiled=True).reshape(2 * pairs, step)]
    ppermute x0 -> x3, waiting for transfers between devices: none -> 13.7 us  [the longest x2 13.7 us: on_device(): lower.append(lax.ppermute(lower[-1] if lower else both, 'row', pairs_2))]
    ppermute x0 -> x3, starting transfers between devices: none -> 4.74 us  [the longest x2 2.54 us: on_device(): lower.append(lax.ppermute(lower[-1] if lower else both, 'row', pairs_2))]
  transfers between devices with their start and end apart: 6 -> 8, of which waited for: 5 -> 5; matrix products, arithmetic and copies ran while one was open for 9% -> 11% of each run, Pallas kernels for 0% -> 0%
where the time goes in v1:
time: 248 us
  waiting for transfers between devices  116 us (47%)
  matrix products  38.8 us (16%)
  blocking collectives  31.2 us (13%)
  other arithmetic  24.6 us (10%)
  between operations  16.5 us (7%)
  starting transfers between devices  14.1 us (6%)
  local copies, waits for them, and re-layouts  6.02 us (2%)
    all_gather x4, waiting for transfers between devices, on_device(): lax.all_gather(piece, 'col', axis=1, tiled=True).reshape(2 * pairs, step)  101 us
    dot_general x16, matrix products, contract(): lax.dot_general(left_side, right_side, (((0,), (0,)), ((), ())), preferre...  38.8 us
    all_gather x1, blocking collectives, on_device(): lax.all_gather(bands, 'col', axis=1, tiled=True).astype(jnp.int32)  31.2 us
    ppermute x2, waiting for transfers between devices, on_device(): lower.append(lax.ppermute(lower[-1] if lower else both, 'row', pairs_2))  13.7 us
    another operation x2, other arithmetic, on_device(): chi_imag = jnp.stack([jnp.concatenate(p, axis=0) for p in imag_parts])  10.8 us
    all_to_all x1, starting transfers between devices, on_device(): lax.all_to_all(spread, 'col', split_axis=2, concat_axis=1, tiled=True)  9.23 us
    another operation x2, other arithmetic, on_device(): chi_real = jnp.stack([jnp.concatenate(p, axis=0) for p in real_parts])  9.18 us
  transfers between devices with their start and end apart: 8, of which 5 were waited for; matrix products, arithmetic and copies ran while one was open for 11% of the time, Pallas kernels for 0%

profile of v1, /device:TPU:1, one launch (start us, length us, event | category | flops | bytes accessed | tf_op | source)
XLA Modules:
  0.0 247.6 jit_solution(5581072987060123237)
XLA Ops:
  11.3 2.5 %collective-permute-start = (bf16[2,16,4096]{2,1,0:T(8,128)(2,1)S(1)}, bf16[2,16,4096]{2,1,0:T(8,128)(2,1)S(1)}, u32[]{:S(2)}, u32[]{:S(2)}) collective-permute-start(bf16[2,16,4096]{2,1,0:T(8,128)(2,1)S(1)} %get-tuple-element.17), channel_id=1, source_target_pairs={{0,32},{32,64},{64,96},{96,0},{1,33},{33,65},{65,97},{97,1},{2,34}... | collective-permute-start | bytes 786440 | tf_op jit(solution)/shard_map/ppermute | solution.py:50
  13.8 2.2 collective-permute-start.2
  16.1 6.0 %collective-permute-done = bf16[2,16,4096]{2,1,0:T(8,128)(2,1)S(1)} collective-permute-done((bf16[2,16,4096]{2,1,0:T(8,128)(2,1)S(1)}, bf16[2,16,4096]{2,1,0:T(8,128)(2,1)S(1)}, u32[]{:S(2)}, u32[]{:S(2)}) %collective-permute-start) | collective-permute-done | bytes 262176 | tf_op jit(solution)/shard_map/ppermute | solution.py:50
  22.0 7.7 %collective-permute-done.1 = bf16[2,16,4096]{2,1,0:T(8,128)(2,1)S(1)} collective-permute-done((bf16[2,16,4096]{2,1,0:T(8,128)(2,1)S(1)}, bf16[2,16,4096]{2,1,0:T(8,128)(2,1)S(1)}, u32[]{:S(2)}, u32[]{:S(2)}) %collective-permute-start.1) | collective-permute-done | bytes 262176 | tf_op jit(solution)/shard_map/ppermute | solution.py:50
  33.8 9.2 %all-to-all-start = ((bf16[2,16,32,512]{3,1,0,2:T(8,128)(2,1)}), bf16[2,16,32,512]{3,1,0,2:T(8,128)(2,1)S(1)}, u32[]{:S(2)}, u32[]{:S(2)}) async-start(bf16[2,16,32,512]{3,1,0,2:T(8,128)(2,1)} %copy.26), calls=%async_computation | async-start | bytes 2097152 | tf_op jit(solution)/shard_map/all_to_all | solution.py:58
  46.7 31.2 %all-gather = f32[32,16,2]{1,2,0:T(2,128)S(1)} all-gather(f32[1,16,2]{1,2,0:T(2,128)S(1)} %fusion.10), channel_id=1, replica_groups=mesh['row'=4,'col'=32] {'col'}, dimensions={0}, use_global_device_ids=true | all-gather | bytes 4224 | tf_op jit(solution)/shard_map/all_gather | solution.py:42
  80.3 4.4 %convolution_convert_fusion.10 = bf16[1024,512]{1,0:T(8,128)(2,1)} fusion(bf16[1024,1024]{1,0:T(8,128)(2,1)} %bitcast.89, bf16[512,512]{1,0:T(8,128)(2,1)S(1)} %get-tuple-element.11, bf16[512,512]{1,0:T(8,128)(2,1)S(1)} %get-tuple-element.18), kind=kOutput, calls=%fused_computation.18 | convolution fusion | flops 1076363264 | bytes 4194304 | tf_op jit(solution)/shard_map/dot_general | solution.py:20
  84.7 24.7 %all-gather.6.cloned.1.call-done = bf16[2,512,1024]{2,1,0:T(8,128)(2,1)} async-done(((bf16[2,16,1024]{2,1,0:T(8,128)(2,1)}), bf16[2,512,1024]{2,1,0:T(8,128)(2,1)}) %all-gather.6.cloned.1.call-update) | async-done | bytes 2097168 | tf_op jit(solution)/shard_map/all_gather | solution.py:75
  109.4 4.0 %convolution_convert_fusion.11 = bf16[1024,512]{1,0:T(8,128)(2,1)} fusion(bf16[1024,1024]{1,0:T(8,128)(2,1)} %bitcast.93, bf16[512,512]{1,0:T(8,128)(2,1)S(1)} %get-tuple-element.11, bf16[512,512]{1,0:T(8,128)(2,1)S(1)} %get-tuple-element.18), kind=kOutput, calls=%fused_computation.19 | convolution fusion | flops 1076363264 | bytes 4194304 | tf_op jit(solution)/shard_map/dot_general | solution.py:20
  115.0 2.5 %convolution_convert_fusion.2 = bf16[1024,512]{1,0:T(8,128)(2,1)S(1)} fusion(bf16[1024,1024]{1,0:T(8,128)(2,1)S(1)} %bitcast.90, bf16[512,512]{1,0:T(8,128)(2,1)} %copy-done.8, bf16[512,512]{1,0:T(8,128)(2,1)} %copy-done.5), kind=kOutput, calls=%fused_computation.10 | convolution fusion | flops 1076363264 | bytes 4194304 | tf_op jit(solution)/shard_map/dot_general | solution.py:20
  117.5 37.3 %all-gather.10.cloned.1.call-done = bf16[2,512,1024]{2,1,0:T(8,128)(2,1)} async-done(((bf16[2,16,1024]{2,1,0:T(8,128)(2,1)}), bf16[2,512,1024]{2,1,0:T(8,128)(2,1)}) %all-gather.10.cloned.1.call-update) | async-done | bytes 2097168 | tf_op jit(solution)/shard_map/all_gather | solution.py:75
  154.8 4.2 %convolution_convert_fusion.9 = bf16[1024,512]{1,0:T(8,128)(2,1)} fusion(bf16[1024,1024]{1,0:T(8,128)(2,1)} %bitcast.97, bf16[512,512]{1,0:T(8,128)(2,1)} %copy-done.5, bf16[512,512]{1,0:T(8,128)(2,1)} %copy-done.11), kind=kOutput, calls=%fused_computation.17 | convolution fusion | flops 1076363264 | bytes 4194304 | tf_op jit(solution)/shard_map/dot_general | solution.py:20
  159.0 2.3 convolution_convert_fusion.1
  161.3 38.7 %all-gather.12.cloned.1.call-done = bf16[2,512,1024]{2,1,0:T(8,128)(2,1)} async-done(((bf16[2,16,1024]{2,1,0:T(8,128)(2,1)}), bf16[2,512,1024]{2,1,0:T(8,128)(2,1)}) %all-gather.12.cloned.1.call-update) | async-done | bytes 2097168 | tf_op jit(solution)/shard_map/all_gather | solution.py:75
  200.0 3.3 %convolution_convert_fusion.8 = bf16[1024,512]{1,0:T(8,128)(2,1)S(1)} fusion(bf16[1024,1024]{1,0:T(8,128)(2,1)} %bitcast.101, bf16[512,512]{1,0:T(8,128)(2,1)} %copy-done.5, bf16[512,512]{1,0:T(8,128)(2,1)} %copy-done.11), kind=kOutput, calls=%fused_computation.16 | convolution fusion | flops 1076363264 | bytes 4194304 | tf_op jit(solution)/shard_map/dot_general | solution.py:20
  203.3 2.3 convolution_convert_fusion
  208.5 2.5 %convolution_convert_fusion.6 = bf16[1024,512]{1,0:T(8,128)(2,1)} fusion(bf16[1024,1024]{1,0:T(8,128)(2,1)S(1)} %bitcast.92, bf16[512,512]{1,0:T(8,128)(2,1)S(1)} %copy-done.4, bf16[512,512]{1,0:T(8,128)(2,1)S(1)} %get-tuple-element.10), kind=kOutput, calls=%fused_computation.14 | convolution fusion | flops 1076363264 | bytes 4194304 | tf_op jit(solution)/shard_map/dot_general | solution.py:20
  211.0 2.3 convolution_convert_fusion.5
  214.6 2.4 convolution_convert_fusion.4
  217.0 2.3 convolution_convert_fusion.7
  221.1 2.8 %maximum_bitcast_fusion = (bf16[1,4096,512]{2,1,0:T(8,128)(2,1)S(1)}, bf16[1,4096,512]{2,1,0:T(8,128)(2,1)}) fusion(bf16[1024,512]{1,0:T(8,128)(2,1)S(1)} %convolution_convert_fusion.12, bf16[1024,512]{1,0:T(8,128)(2,1)S(1)} %convolution_convert_fusion.13, bf16[1024,512]{1,0:T(8,128)(2,1)S(1)} %convolution_convert_fusion.14, ...), kind=kLoop, calls=%fused_computation.3 | loop fusion | flops 33554432 | bytes 16777216 | tf_op jit(solution)/shard_map/stack | solution.py:79
  224.0 6.3 %pad_maximum_fusion = bf16[2,4096,512]{2,1,0:T(8,128)(2,1)} fusion(bf16[1,4096,512]{2,1,0:T(8,128)(2,1)} %get-tuple-element.29, bf16[1,4096,512]{2,1,0:T(8,128)(2,1)S(1)} %get-tuple-element.28), kind=kLoop, calls=%fused_computation.1 | loop fusion | flops 4194304 | bytes 16777216 | tf_op jit(solution)/shard_map/stack | solution.py:79
  230.3 4.4 %maximum_bitcast_fusion.2 = (bf16[1,4096,512]{2,1,0:T(8,128)(2,1)S(1)}, bf16[1,4096,512]{2,1,0:T(8,128)(2,1)}) fusion(bf16[1024,512]{1,0:T(8,128)(2,1)} %convolution_convert_fusion.4, bf16[1024,512]{1,0:T(8,128)(2,1)} %convolution_convert_fusion.5, bf16[1024,512]{1,0:T(8,128)(2,1)} %convolution_convert_fusion.6, ...), kind=kLoop, calls=%fused_computation.5 | loop fusion | flops 33554432 | bytes 16777216 | tf_op jit(solution)/shard_map/stack | solution.py:80
  234.8 6.3 %pad_maximum_fusion.1 = bf16[2,4096,512]{2,1,0:T(8,128)(2,1)} fusion(bf16[1,4096,512]{2,1,0:T(8,128)(2,1)} %get-tuple-element.31, bf16[1,4096,512]{2,1,0:T(8,128)(2,1)S(1)} %get-tuple-element.30), kind=kLoop, calls=%fused_computation.2 | loop fusion | flops 4194304 | bytes 16777216 | tf_op jit(solution)/shard_map/stack | solution.py:80
  (87 shorter events, 19.2 us)
Async XLA Ops:
  7.2 73.1 %all-gather.8.cloned.1.call-start = ((), (), s32[]{:S(2)}) async-start(), calls=%async_computation.2 | async-start | bytes 2162688 | tf_op jit(solution)/shard_map/all_gather | solution.py:75
  8.8 100.6 %all-gather.6.cloned.1.call-start = ((), (), s32[]{:S(2)}) async-start(), calls=%async_computation.1 | async-start | bytes 2162688 | tf_op jit(solution)/shard_map/all_gather | solution.py:75
  9.6 145.2 %all-gather.10.cloned.1.call-start = ((), (), s32[]{:S(2)}) async-start(), calls=%async_computation.3 | async-start | bytes 2162688 | tf_op jit(solution)/shard_map/all_gather | solution.py:75
  11.3 10.7 %collective-permute-start = (bf16[2,16,4096]{2,1,0:T(8,128)(2,1)S(1)}, bf16[2,16,4096]{2,1,0:T(8,128)(2,1)S(1)}, u32[]{:S(2)}, u32[]{:S(2)}) collective-permute-start(bf16[2,16,4096]{2,1,0:T(8,128)(2,1)S(1)} %get-tuple-element.17), channel_id=1, source_target_pairs={{0,32},{32,64},{64,96},{96,0},{1,33},{33,65},{65,97},{97,1},{2,34}... | collective-permute-start | bytes 786440 | tf_op jit(solution)/shard_map/ppermute | solution.py:50
  13.8 8.2 %collective-permute-start.2 = (bf16[2,16,4096]{2,1,0:T(8,128)(2,1)S(1)}, bf16[2,16,4096]{2,1,0:T(8,128)(2,1)S(1)}, u32[]{:S(2)}, u32[]{:S(2)}) collective-permute-start(bf16[2,16,4096]{2,1,0:T(8,128)(2,1)S(1)} %get-tuple-element.17), channel_id=1, source_target_pairs={{32,0},{64,32},{96,64},{0,96},{33,1},{65,33},{97,65},{1,97},{34,2}... | collective-permute-start | bytes 786440 | tf_op jit(solution)/shard_map/ppermute | solution.py:52
  22.0 7.8 %collective-permute-start.1 = (bf16[2,16,4096]{2,1,0:T(8,128)(2,1)S(1)}, bf16[2,16,4096]{2,1,0:T(8,128)(2,1)S(1)}, u32[]{:S(2)}, u32[]{:S(2)}) collective-permute-start(bf16[2,16,4096]{2,1,0:T(8,128)(2,1)S(1)} %collective-permute-done), channel_id=1, source_target_pairs={{0,32},{32,64},{64,96},{96,0},{1,33},{33,65},{65,97},{97,1},{2,34}... | collective-permute-start | bytes 786440 | tf_op jit(solution)/shard_map/ppermute | solution.py:50
  32.2 11.4 %copy-start.12 = (f32[2]{0:T(128)S(1)}, f32[2]{0:T(128)}, u32[]{:S(2)}) copy-start(f32[2]{0:T(128)} %param.13) | copy-start | bytes 28
  32.2 14.5 %copy-start.15 = (s32[16]{0:T(128)S(1)}, s32[16]{0:T(128)}, u32[]{:S(2)}) copy-start(s32[16]{0:T(128)} %param.10) | copy-start | bytes 196
  32.2 14.5 %copy-start.16 = (s32[16]{0:T(128)S(1)}, s32[16]{0:T(128)}, u32[]{:S(2)}) copy-start(s32[16]{0:T(128)} %param.9) | copy-start | bytes 196
  32.2 45.9 %copy-start.13 = (f32[16]{0:T(128)S(1)}, f32[16]{0:T(128)}, u32[]{:S(2)}) copy-start(f32[16]{0:T(128)} %param.11) | copy-start | bytes 196
  32.2 46.0 %copy-start.14 = (f32[32]{0:T(128)S(1)}, f32[32]{0:T(128)}, u32[]{:S(2)}) copy-start(f32[32]{0:T(128)} %param.12) | copy-start | bytes 388
  33.8 44.6 %all-to-all-start = ((bf16[2,16,32,512]{3,1,0,2:T(8,128)(2,1)}), bf16[2,16,32,512]{3,1,0,2:T(8,128)(2,1)S(1)}, u32[]{:S(2)}, u32[]{:S(2)}) async-start(bf16[2,16,32,512]{3,1,0,2:T(8,128)(2,1)} %copy.26), calls=%async_computation | async-start | bytes 2097152 | tf_op jit(solution)/shard_map/all_to_all | solution.py:58
  43.0 157.0 %all-gather.12.cloned.1.call-start = ((), (), s32[]{:S(2)}) async-start(), calls=%async_computation.4 | async-start | bytes 2162688 | tf_op jit(solution)/shard_map/all_gather | solution.py:75
  80.3 29.1 %copy-start.11 = (bf16[512,512]{1,0:T(8,128)(2,1)}, bf16[512,512]{1,0:T(8,128)(2,1)S(1)}, u32[]{:S(2)}) copy-start(bf16[512,512]{1,0:T(8,128)(2,1)S(1)} %get-tuple-element.18) | copy-start | bytes 1572868
  80.3 33.2 %copy-start.5 = (bf16[512,512]{1,0:T(8,128)(2,1)}, bf16[512,512]{1,0:T(8,128)(2,1)S(1)}, u32[]{:S(2)}) copy-start(bf16[512,512]{1,0:T(8,128)(2,1)S(1)} %get-tuple-element.11) | copy-start | bytes 1572868
  80.3 33.2 %copy-start.8 = (bf16[512,512]{1,0:T(8,128)(2,1)}, bf16[512,512]{1,0:T(8,128)(2,1)S(1)}, u32[]{:S(2)}) copy-start(bf16[512,512]{1,0:T(8,128)(2,1)S(1)} %get-tuple-element.19) | copy-start | bytes 1572868
  109.4 4.0 %copy-start.19 = (bf16[2,512,1024]{2,1,0:T(8,128)(2,1)S(1)}, bf16[2,512,1024]{2,1,0:T(8,128)(2,1)}, u32[]{:S(2)}) copy-start(bf16[2,512,1024]{2,1,0:T(8,128)(2,1)} %all-gather.6.cloned.1.call-done) | copy-start | bytes 6291460
  154.8 4.2 %copy-start.6 = (bf16[512,512]{1,0:T(8,128)(2,1)S(1)}, bf16[512,512]{1,0:T(8,128)(2,1)}, u32[]{:S(2)}) copy-start(bf16[512,512]{1,0:T(8,128)(2,1)} %copy-done.5) | copy-start | bytes 1572868
  154.8 4.2 %copy-start.9 = (bf16[512,512]{1,0:T(8,128)(2,1)S(1)}, bf16[512,512]{1,0:T(8,128)(2,1)}, u32[]{:S(2)}) copy-start(bf16[512,512]{1,0:T(8,128)(2,1)} %copy-done.8) | copy-start | bytes 1572868
  154.8 4.2 %copy-start.21 = (bf16[2,512,1024]{2,1,0:T(8,128)(2,1)S(1)}, bf16[2,512,1024]{2,1,0:T(8,128)(2,1)}, u32[]{:S(2)}) copy-start(bf16[2,512,1024]{2,1,0:T(8,128)(2,1)} %all-gather.10.cloned.1.call-done) | copy-start | bytes 6291460
  200.0 3.3 %copy-start.7 = (bf16[512,512]{1,0:T(8,128)(2,1)S(1)}, bf16[512,512]{1,0:T(8,128)(2,1)}, u32[]{:S(2)}) copy-start(bf16[512,512]{1,0:T(8,128)(2,1)} %copy-done.5) | copy-start | bytes 1572868
  200.0 3.3 %copy-start.10 = (bf16[512,512]{1,0:T(8,128)(2,1)S(1)}, bf16[512,512]{1,0:T(8,128)(2,1)}, u32[]{:S(2)}) copy-start(bf16[512,512]{1,0:T(8,128)(2,1)} %copy-done.8) | copy-start | bytes 1572868
  200.0 3.3 %copy-start.23 = (bf16[2,512,1024]{2,1,0:T(8,128)(2,1)S(1)}, bf16[2,512,1024]{2,1,0:T(8,128)(2,1)}, u32[]{:S(2)}) copy-start(bf16[2,512,1024]{2,1,0:T(8,128)(2,1)} %all-gather.12.cloned.1.call-done) | copy-start | bytes 6291460
  214.6 2.4 copy-start.20
  (8 other events, 13.7 us)
Sparse Core Ops, SparseCore 0:
  10.9 55.1 all-gather.7
  68.5 40.8 all-gather.5
  111.8 42.9 all-gather.9
  157.0 42.9 all-gather.11
